TPU v7x, 32 devices: a whole 2x2x4 slice. The times are simulated.
32 devices in a mesh: req: 4 (over y, x), head: 4 (over z), dev: 2 (over core).
Axes of the slice: x: 2, y: 2, z: 4, core: 2. Of those that a mesh axis runs over, the one named last changes fastest.
Arguments:
- tokens: bfloat16 [4, 512, 2304], P('req', 'dev')
- attn_gain: float32 [2304], replicated, may hold values from 0.1 to 1.9
- w_qkv: bfloat16 [2304, 3, 2048], P(None, None, 'head')
- w_out: bfloat16 [2048, 2304], P('head'), may hold values from -0.125 to 0.125
- moe_gain: float32 [2304], replicated, may hold values from 0.1 to 1.9
- routes: int32 [4, 512, 2], P(None, 'dev'), may hold values from 0 to 7, all different within a row; in each aligned block of 256 rows (0 to 255, 256 to 511, ..., all dimensions but the last counted through in order) at most 96 rows name the same one
- route_weight: float32 [4, 512, 2], P(None, 'dev'), may hold values from 0.2 to 1
- w_gate_up: bfloat16 [8, 2, 2304, 5760], P('head', None, None, 'req'), may hold values from -0.125 to 0.125
- w_down: bfloat16 [8, 5760, 2304], P('head', 'req'), may hold values from -0.078125 to 0.078125
- kv_cache: bfloat16 [4, 16, 128, 2, 2048], P('req', None, 'dev', None, 'head'), may hold values from -6 to 6
- lengths: int32 [4], replicated, may hold values from 1 to 2048, as said below
- block_owner: int32 [4, 16], replicated, may hold values from 0 to 3, as said below
- block_slot: int32 [4, 16], replicated, may hold values from 0 to 15, as said below
Outputs:
- layer_out: bfloat16 [4, 2, 256, 2304], P('req', 'dev', 'head')
- page_pool: bfloat16 [64, 128, 2, 2048], P('req', 'dev', None, 'head')
Inputs may be any that keep to these rules, and one draw needn't show every extreme that they name: `routes`: in each aligned block of 256 rows (the rows of one device) no expert is named more than 96 times; the other loads are skewed. `lengths`: each request has a length of 1 or more tokens; some request has exactly 2048. `block_owner`: each holder holds exactly 4 pages of every request. The pairs of block_owner and block_slot are distinct over all pages of all requests.
All inputs are finite; a program needn't handle non-finite values.
Results may differ from a plain program's by a relative error of at most 0.012.
Values may be sent and summed in bfloat16 or wider, within the bound.
No kernel may reach another device: no remote copies, remote signals or barrier semaphores. Data moves between devices by JAX's collectives and lax.ppermute only.
A program may use at most 192 MiB of HBM per device.

v0:
```python
import jax
import jax.numpy as jnp
from jax import lax
from jax.sharding import PartitionSpec as P

EXPERTS = 8
HD = 64


def shifted(block, axis, distance):
    devices = range(lax.axis_size(axis))
    route = [(i - distance, i) for i in devices if i - distance in devices]
    return lax.ppermute(block, axis, route)


def norm_rows(values, gain_vec):
    widened = values.astype(jnp.float32)
    inv_rms = lax.rsqrt(jnp.mean(widened * widened, axis=-1, keepdims=True) + 1e-05)
    return (widened * inv_rms * gain_vec).astype(jnp.bfloat16)


def rotate(values, positions):
    half_dim = values.shape[-1] // 2
    frequency = 10000.0 ** (-jnp.arange(half_dim, dtype=jnp.float32) / half_dim)
    angles = positions[:, None] * frequency[None, :]
    cosine = jnp.cos(angles)[:, None, :]
    sine_part = jnp.sin(angles)[:, None, :]
    front_half = values[..., :half_dim]
    back_half = values[..., half_dim:]
    return jnp.concatenate(
        [front_half * cosine - back_half * sine_part, back_half * cosine + front_half * sine_part],
        axis=-1,
    )


def slot_tables(route_ids, weights, first_expert, experts_here, capacity):
    expert_ids = first_expert + jnp.arange(experts_here, dtype=jnp.int32)
    matches = (route_ids[..., None] == expert_ids).astype(jnp.float32)
    hit_shape = matches.shape
    flat_hits = matches.reshape(hit_shape[:-3] + (hit_shape[-3] * hit_shape[-2], hit_shape[-1]))
    ranking = (jnp.cumsum(flat_hits, axis=-2) - flat_hits).reshape(hit_shape)
    places = (ranking[..., None] == jnp.arange(capacity, dtype=jnp.float32)).astype(
        jnp.float32
    ) * matches[..., None]
    dispatch = jnp.sum(places, axis=-3)
    combine = jnp.sum(places * weights[..., None, None], axis=-3)
    return (dispatch, combine)


def body(
    tokens,
    attn_gain,
    w_qkv,
    w_out,
    moe_gain,
    routes,
    route_weight,
    w_gate_up,
    w_down,
    kv_cache,
    lengths,
    block_owner,
    block_slot,
):
    half_rows = tokens.shape[1]
    model_width = tokens.shape[2]
    dev_index = lax.axis_index("dev")
    req_index = lax.axis_index("req")
    head_index = lax.axis_index("head")
    local_cols = w_qkv.shape[2]
    head_count = local_cols // HD
    normed = norm_rows(tokens[0], attn_gain)
    projected = jnp.dot(
        normed, w_qkv.reshape(model_width, 3 * local_cols), preferred_element_type=jnp.float32
    ).reshape(half_rows, 3, head_count, HD)
    query_pos = dev_index * half_rows + jnp.arange(half_rows, dtype=jnp.int32)
    angles_at = query_pos.astype(jnp.float32)
    queries = rotate(projected[:, 0], angles_at).astype(jnp.bfloat16)
    key_rows = rotate(projected[:, 1], angles_at).astype(jnp.bfloat16)
    values = projected[:, 2].astype(jnp.bfloat16)
    earlier_keys, earlier_values = shifted((key_rows, values), "dev", 1)
    all_keys = jnp.concatenate([earlier_keys, key_rows], axis=0)
    all_values = jnp.concatenate([earlier_values, values], axis=0)
    key_pos = (dev_index - 1) * half_rows + jnp.arange(2 * half_rows, dtype=jnp.int32)
    allowed = (key_pos[None, :] <= query_pos[:, None]) & (key_pos[None, :] >= 0)
    scores = (
        jnp.einsum("qhd,khd->hqk", queries, all_keys, preferred_element_type=jnp.float32) * 0.125
    )
    scores = jnp.where(allowed[None], scores, -1e30)
    row_peak = jnp.max(scores, axis=-1, keepdims=True)
    exp_scores = jnp.exp(scores - row_peak)
    row_total = jnp.sum(exp_scores, axis=-1)
    attended = (
        jnp.einsum(
            "hqk,khd->qhd",
            exp_scores.astype(jnp.bfloat16),
            all_values,
            preferred_element_type=jnp.float32,
        )
        / jnp.transpose(row_total)[:, :, None]
    )
    attended = attended.astype(jnp.bfloat16).reshape(half_rows, local_cols)
    partial_value = jnp.dot(attended, w_out, preferred_element_type=jnp.float32)
    attn_mixed = lax.psum(partial_value.astype(jnp.bfloat16), "head").astype(jnp.float32)
    residual = (tokens[0].astype(jnp.float32) + attn_mixed).astype(jnp.bfloat16)
    moe_in = norm_rows(residual, moe_gain)
    experts_here = w_gate_up.shape[0]
    first_expert = head_index * experts_here
    top_count = routes.shape[2]
    capacity = half_rows * top_count * 3 // (2 * EXPERTS)
    own_routes = lax.dynamic_index_in_dim(routes, req_index, 0, keepdims=True)
    own_weights = lax.dynamic_index_in_dim(route_weight, req_index, 0, keepdims=True)
    own_dispatch, own_combine = slot_tables(
        own_routes, own_weights, first_expert, experts_here, capacity
    )
    own_dispatch = own_dispatch[0]
    own_combine = own_combine[0]
    picked_own = jnp.einsum(
        "tec,td->ced", own_dispatch.astype(jnp.bfloat16), moe_in, preferred_element_type=jnp.float32
    ).astype(jnp.bfloat16)
    req_total = lax.axis_size("req")
    dev_total = lax.axis_size("dev")
    split = dev_total > 1 and experts_here % dev_total == 0
    per_core = experts_here // dev_total if split else experts_here
    if split:
        first_here = dev_index * per_core
        gate_up_here = lax.dynamic_slice_in_dim(w_gate_up, first_here, per_core, 0)
        down_here = lax.dynamic_slice_in_dim(w_down, first_here, per_core, 0)
        rows_here = lax.all_to_all(picked_own, "dev", split_axis=1, concat_axis=0, tiled=True)
    else:
        gate_up_here, down_here, rows_here = (w_gate_up, w_down, picked_own)

    def partner_move(block, step):
        return lax.ppermute(block, "req", [(i, i ^ step) for i in range(req_total)])

    def experts_on(rows):
        groups = rows.shape[0]
        flat = rows.reshape(groups * rows.shape[1], per_core, model_width)
        both = jnp.einsum("ned,egdf->gnef", flat, gate_up_here, preferred_element_type=jnp.float32)
        hidden = (jax.nn.silu(both[0]) * both[1]).astype(jnp.bfloat16)
        down = jnp.einsum("nef,efd->ned", hidden, down_here, preferred_element_type=jnp.float32)
        return down.astype(jnp.bfloat16).reshape(rows.shape)

    arrived = {0: rows_here}
    for step in range(1, req_total):
        if step == 3:
            arrived[step] = partner_move(arrived[1], 2)
        else:
            arrived[step] = partner_move(rows_here, step)
    plan = [[0], [1, 2]] + ([list(range(3, req_total))] if req_total > 3 else [])
    plan = [[k for k in group if k < req_total] for group in plan]
    returned = []
    for group in plan:
        if not group:
            continue
        outs = experts_on(jnp.stack([arrived[k] for k in group], axis=0))
        for slot_index, step in enumerate(group):
            part = outs[slot_index]
            part = part if step == 0 else partner_move(part, step)
            if split:
                part = lax.all_to_all(part, "dev", split_axis=0, concat_axis=1, tiled=True)
            returned.append(part)
    token_weights = jnp.sum(own_combine, axis=-1)
    dispatch_bf = own_dispatch.astype(jnp.bfloat16)
    selected = sum(
        (
            jnp.einsum("tec,ced->ted", dispatch_bf, part, preferred_element_type=jnp.float32)
            for part in returned
        )
    )
    moe_out = jnp.sum(token_weights[:, :, None] * selected, axis=1)
    summed = lax.psum_scatter(
        moe_out.astype(jnp.bfloat16), "head", scatter_dimension=0, tiled=True
    ).astype(jnp.float32)
    rows_out = summed.shape[0]
    kept_rows = lax.dynamic_slice_in_dim(residual, head_index * rows_out, rows_out, 0)
    layer_out = (
        (kept_rows.astype(jnp.float32) + summed)
        .astype(jnp.bfloat16)
        .reshape(1, 1, rows_out, model_width)
    )
    owners_total = lax.axis_size("req")
    block_total = block_owner.shape[1]
    finished_total = block_owner.shape[0]
    per_owner = block_total // owners_total
    block_ids = jnp.arange(block_total, dtype=jnp.int32)
    same_owner = block_owner[:, :, None] == block_owner[:, None, :]
    before_mask = block_ids[None, :] < block_ids[:, None]
    page_rank = jnp.sum((same_owner & before_mask[None]).astype(jnp.int32), axis=2)
    own_owner = lax.dynamic_index_in_dim(block_owner, req_index, 0, keepdims=False)
    own_rank = lax.dynamic_index_in_dim(page_rank, req_index, 0, keepdims=False)
    dest_place = own_owner * per_owner + own_rank
    source_block = jnp.sum(
        jnp.where(dest_place[None, :] == block_ids[:, None], block_ids[None, :], 0), axis=1
    )
    page_half = kv_cache.shape[2]
    page_size = page_half * lax.axis_size("dev")
    token_pos = (
        block_ids[:, None] * page_size
        + dev_index * page_half
        + jnp.arange(page_half, dtype=jnp.int32)[None, :]
    )
    own_length = lax.dynamic_index_in_dim(lengths, req_index, 0, keepdims=False)
    live_cache = jnp.where(
        (token_pos < own_length)[:, :, None, None], kv_cache[0], jnp.zeros((), jnp.bfloat16)
    )
    outgoing = jnp.take(live_cache, source_block, axis=0)
    received = lax.all_to_all(outgoing, "req", split_axis=0, concat_axis=0, tiled=True)
    request_ids = jnp.arange(finished_total, dtype=jnp.int32)
    arrive_place = request_ids[:, None] * per_owner + page_rank
    own_blocks = block_owner == req_index
    slot_match = own_blocks[None] & (block_slot[None] == block_ids[:, None, None])
    gather_place = jnp.sum(jnp.where(slot_match, arrive_place[None], 0), axis=(1, 2))
    page_pool = jnp.take(received, gather_place, axis=0)
    return (layer_out, page_pool)


def solution(mesh):
    return jax.shard_map(
        body,
        mesh=mesh,
        in_specs=(
            P("req", "dev", None),
            P(),
            P(None, None, "head"),
            P("head", None),
            P(),
            P(None, "dev", None),
            P(None, "dev", None),
            P("head", None, None, "req"),
            P("head", "req", None),
            P("req", None, "dev", None, "head"),
            P(),
            P(),
            P(),
        ),
        out_specs=(P("req", "dev", "head", None), P("req", "dev", None, "head")),
        check_vma=False,
    )
```

profile of v0, /device:TPU:0, one launch (start us, length us, event | category | flops | bytes accessed | tf_op | source)
XLA Modules:
  0.0 311.2 jit_solution(5563176906753510006)
XLA Ops:
  7.3 9.9 %copy.53 = bf16[2304,3,512]{0,2,1:T(8,128)(2,1)} copy(bf16[2304,3,512]{2,0,1:T(8,128)(2,1)} %param.17) | data formatting | bytes 14155776 | tf_op args[2]
  17.5 5.2 %fusion.68 = f32[256,3,8,64]{0,3,2,1:T(8,128)S(1)} fusion(bf16[3,8,64,2304]{3,2,1,0:T(8,128)(2,1)} %bitcast.186, bf16[1,256,2304]{2,1,0:T(8,128)(2,1)S(1)} %copy-done.2, f32[2304]{0:T(1024)} %param.16, f32[256]{0:T(256)S(1)} %add_rsqrt_fusion.1), kind=kOutput, calls=%fused_computation.64 | convolution fusion | flops 1814298624 | bytes 9840640 | tf_op jit(solution)/shard_map/dot_general | solution.py:73
  23.2 3.1 collective-permute-start.1
  40.7 55.2 %all-reduce.2.cloned.1.call-done = bf16[256,2304]{1,0:T(8,128)(2,1)} async-done(((bf16[256,2304]{1,0:T(8,128)(2,1)}), bf16[256,2304]{1,0:T(8,128)(2,1)}) %all-reduce.2.cloned.1.call-update) | async-done | bytes 1179664 | tf_op jit(solution)/shard_map/psum | solution.py:104
  98.4 5.4 %all_to_all.95 = bf16[96,2,2304]{2,0,1:T(8,128)(2,1)} all-to-all(bf16[96,2,2304]{2,0,1:T(8,128)(2,1)S(1)} %convert_bitcast_fusion.1), channel_id=1, replica_groups=mesh['req'=4,'head'=4,'dev'=2] {'dev'}, dimensions={1} | all-to-all | bytes 1769472 | tf_op jit(solution)/shard_map/all_to_all | solution.py:129
  111.3 14.4 %collective-permute-done.2 = bf16[192,1,2304]{2,0,1:T(8,128)(2,1)} collective-permute-done((bf16[192,1,2304]{2,0,1:T(8,128)(2,1)}, bf16[192,1,2304]{2,0,1:T(8,128)(2,1)}, u32[]{:S(2)}, u32[]{:S(2)}) %collective-permute-start.2) | collective-permute-done | bytes 884768 | tf_op jit(solution)/shard_map/ppermute | solution.py:134
  128.8 9.9 %fusion.26 = f32[2,384,1,1440]{1,3,0,2:T(8,128)S(1)} fusion(bf16[384,2304,1]{1,0,2:T(8,128)(2,1)S(1)} %bitcast.193, bf16[2,2,2304,1440]{2,3,1,0:T(8,128)(2,1)} %param.22, s32[]{:T(128)S(6)} %select_n.44), kind=kOutput, calls=%fused_computation.30 | convolution fusion | flops 5096079360 | bytes 19464196 | tf_op jit(solution)/shard_map/ned,egdf->gnef/dot_general | solution.py:139
  138.7 3.0 fusion.23
  145.7 7.6 %fusion.44 = f32[2,192,1,1440]{3,1,0,2:T(8,128)S(1)} fusion(bf16[192,2304,1]{1,0,2:T(8,128)(2,1)} %bitcast.26, bf16[2,2,2304,1440]{2,3,1,0:T(8,128)(2,1)} %param.22, s32[]{:T(128)S(6)} %select_n.44), kind=kOutput, calls=%fused_computation.38 | convolution fusion | flops 2548039680 | bytes 16367620 | tf_op jit(solution)/shard_map/ned,egdf->gnef/dot_general | solution.py:139
  156.4 3.1 %reduce.7 = bf16[192,2304]{1,0:T(8,128)(2,1)} reduce(bf16[192,1,2304]{2,0,1:T(8,128)(2,1)} %fusion.36, bf16[]{:T(256)} %broadcast.399), dimensions={1}, to_apply=%copy.56.reduce_sub_computation | reduce | bytes 1769474 | tf_op jit(solution)/shard_map/convert_element_type | solution.py:142
  161.5 6.4 %all_to_all.96 = bf16[2,2,110592]{2,1,0:T(2,128)(2,1)} all-to-all(bf16[2,2,110592]{2,1,0:T(2,128)(2,1)} %reshape.485), channel_id=1, replica_groups=mesh['req'=4,'head'=4,'dev'=2] {'dev'}, dimensions={0} | all-to-all | bytes 1769472 | tf_op jit(solution)/shard_map/all_to_all | solution.py:161
  175.2 3.1 %reduce.8 = bf16[192,2304]{1,0:T(8,128)(2,1)} reduce(bf16[192,1,2304]{2,0,1:T(8,128)(2,1)} %collective-permute-done.4, bf16[]{:T(256)} %broadcast.399), dimensions={1}, to_apply=%copy.57.reduce_sub_computation | reduce | bytes 1769474 | tf_op jit(solution)/shard_map/ppermute | solution.py:134
  180.4 6.5 %all_to_all.97 = bf16[2,2,110592]{2,1,0:T(2,128)(2,1)} all-to-all(bf16[2,2,110592]{2,1,0:T(2,128)(2,1)} %reshape.487), channel_id=1, replica_groups=mesh['req'=4,'head'=4,'dev'=2] {'dev'}, dimensions={0} | all-to-all | bytes 1769472 | tf_op jit(solution)/shard_map/all_to_all | solution.py:161
  192.1 3.1 %reduce.9 = bf16[192,2304]{1,0:T(8,128)(2,1)} reduce(bf16[192,1,2304]{2,0,1:T(8,128)(2,1)} %collective-permute-done.5, bf16[]{:T(256)} %broadcast.399), dimensions={1}, to_apply=%copy.58.reduce_sub_computation | reduce | bytes 1769474 | tf_op jit(solution)/shard_map/ppermute | solution.py:134
  197.3 6.4 %all_to_all.98 = bf16[2,2,110592]{2,1,0:T(2,128)(2,1)} all-to-all(bf16[2,2,110592]{2,1,0:T(2,128)(2,1)} %reshape.489), channel_id=1, replica_groups=mesh['req'=4,'head'=4,'dev'=2] {'dev'}, dimensions={0} | all-to-all | bytes 1769472 | tf_op jit(solution)/shard_map/all_to_all | solution.py:161
  208.2 8.4 %fusion.47 = f32[2,192,1,1440]{3,1,0,2:T(8,128)S(1)} fusion(bf16[2,2,2304,1440]{2,3,1,0:T(8,128)(2,1)} %param.22, s32[]{:T(128)S(6)} %select_n.44, bf16[192,1,2304]{2,0,1:T(8,128)(2,1)} %collective-permute-done.6), kind=kOutput, calls=%fused_computation.39 | convolution fusion | flops 2548039680 | bytes 16367620 | tf_op jit(solution)/shard_map/ned,egdf->gnef/dot_general | solution.py:139
  222.1 3.0 convolution_add_fusion.1
  225.1 16.5 %collective-permute-done.7 = bf16[192,1,2304]{2,0,1:T(8,128)(2,1)} collective-permute-done((bf16[192,1,2304]{2,0,1:T(8,128)(2,1)S(1)}, bf16[192,1,2304]{2,0,1:T(8,128)(2,1)}, u32[]{:S(2)}, u32[]{:S(2)}) %collective-permute-start.7) | collective-permute-done | bytes 884768 | tf_op jit(solution)/shard_map/ppermute | solution.py:134
  241.6 3.1 %reduce.10 = bf16[192,2304]{1,0:T(8,128)(2,1)} reduce(bf16[192,1,2304]{2,0,1:T(8,128)(2,1)} %collective-permute-done.7, bf16[]{:T(256)} %broadcast.399), dimensions={1}, to_apply=%copy.59.reduce_sub_computation | reduce | bytes 1769474 | tf_op jit(solution)/shard_map/ppermute | solution.py:134
  246.8 6.4 %all_to_all.99 = bf16[2,2,110592]{2,1,0:T(2,128)(2,1)} all-to-all(bf16[2,2,110592]{2,1,0:T(2,128)(2,1)} %reshape.491), channel_id=1, replica_groups=mesh['req'=4,'head'=4,'dev'=2] {'dev'}, dimensions={0} | all-to-all | bytes 1769472 | tf_op jit(solution)/shard_map/all_to_all | solution.py:161
  257.5 4.5 %fusion.63 = bf16[256,2304]{0,1:T(8,128)(2,1)} fusion(f32[2,2304,256]{2,1,0:T(8,128)} %convolution_add_fusion.1, bf16[96,2,2304]{2,0,1:T(8,128)(2,1)S(1)} %bitcast.191, bf16[256,2,96]{0,2,1:T(8,128)(2,1)S(1)} %get-tuple-element.14, f32[256,2]{0,1:T(2,128)S(1)} %get-tuple-element.13), kind=kOutput, calls=%fused_computation.60 | convolution fusion | flops 229441536 | bytes 6883328 | tf_op jit(solution)/shard_map/tec,ced->ted/dot_general | solution.py:167
  266.0 3.8 %all-to-all-start.5 = ((bf16[16,64,2,512]{3,1,2,0:T(8,128)(2,1)}), bf16[16,64,2,512]{3,1,2,0:T(8,128)(2,1)S(1)}, u32[]{:S(2)}, u32[]{:S(2)}) async-start(bf16[16,64,2,512]{3,1,2,0:T(8,128)(2,1)} %broadcast_select_fusion.1), calls=%async_computation.6 | async-start | bytes 4194304 | tf_op jit(solution)/shard_map/all_to_all | solution.py:208
  270.0 25.1 %all-to-all-done.5 = bf16[16,64,2,512]{3,1,2,0:T(8,128)(2,1)S(1)} async-done(((bf16[16,64,2,512]{3,1,2,0:T(8,128)(2,1)}), bf16[16,64,2,512]{3,1,2,0:T(8,128)(2,1)S(1)}, u32[]{:S(2)}, u32[]{:S(2)}) %all-to-all-start.5) | async-done | bytes 2097184 | tf_op jit(solution)/shard_map/all_to_all | solution.py:208
  299.1 3.5 %copy.62 = bf16[16,64,2,512]{3,2,1,0:T(2,128)(2,1)} copy(bf16[16,64,2,512]{3,1,2,0:T(8,128)(2,1)S(1)} %broadcast_select_fusion) | data formatting | bytes 4194304
  (145 shorter events, 80.1 us)
Async XLA Ops:
  7.2 28.7 %copy-start = (bf16[512,2304]{1,0:T(8,128)(2,1)S(1)}, bf16[512,2304]{1,0:T(8,128)(2,1)}, u32[]{:S(2)}) copy-start(bf16[512,2304]{1,0:T(8,128)(2,1)} %param.18) | copy-start | bytes 7077892
  7.2 88.7 %all-reduce.2.cloned.1.call-start = ((), (), s32[]{:S(2)}) async-start(), calls=%async_computation.7 | async-start | bytes 2359296 | tf_op jit(solution)/shard_map/psum | solution.py:104
  7.3 9.9 %copy-start.2 = (bf16[1,256,2304]{2,1,0:T(8,128)(2,1)S(1)}, bf16[1,256,2304]{2,1,0:T(8,128)(2,1)}, u32[]{:S(2)}) copy-start(bf16[1,256,2304]{2,1,0:T(8,128)(2,1)} %param.15) | copy-start | bytes 3538948
  23.2 7.4 %collective-permute-start.1 = (bf16[256,8,64]{0,2,1:T(8,128)(2,1)S(1)}, bf16[256,8,64]{0,2,1:T(8,128)(2,1)}, u32[]{:S(2)}, u32[]{:S(2)}) collective-permute-start(bf16[256,8,64]{0,2,1:T(8,128)(2,1)S(1)} %pad_maximum_fusion.1), channel_id=1, source_target_pairs={{0,1},{2,3},{4,5},{6,7},{8,9},{10,11},{12,13},{14,15},{16,17},{18,... | collective-permute-start | bytes 786440 | tf_op jit(solution)/shard_map/ppermute | solution.py:13
  26.2 7.5 %collective-permute-start = (bf16[256,8,64]{0,2,1:T(8,128)(2,1)S(1)}, bf16[256,8,64]{0,2,1:T(8,128)(2,1)}, u32[]{:S(2)}, u32[]{:S(2)}) collective-permute-start(bf16[256,8,64]{0,2,1:T(8,128)(2,1)S(1)} %fusion.102), channel_id=1, source_target_pairs={{0,1},{2,3},{4,5},{6,7},{8,9},{10,11},{12,13},{14,15},{16,17},{18,... | collective-permute-start | bytes 786440 | tf_op jit(solution)/shard_map/ppermute | solution.py:13
  37.8 58.2 %copy-start.3 = (bf16[1,256,2304]{2,1,0:T(8,128)(2,1)S(1)}, bf16[1,256,2304]{2,1,0:T(8,128)(2,1)}, u32[]{:S(2)}) copy-start(bf16[1,256,2304]{2,1,0:T(8,128)(2,1)} %param.15) | copy-start | bytes 3538948
  37.8 59.9 %copy-start.7 = (f32[2304]{0:T(1024)S(1)}, f32[2304]{0:T(1024)}, u32[]{:S(2)}) copy-start(f32[2304]{0:T(1024)} %param.19) | copy-start | bytes 27652
  37.8 264.8 %reduce-scatter.2.cloned.1.call-start = ((), (), s32[]{:S(2)}) async-start(), calls=%async_computation.8 | async-start | bytes 1474560 | tf_op jit(solution)/shard_map/reduce_scatter | solution.py:172
  98.3 9.2 %copy-start.5 = (bf16[1,16,64,2,512]{4,3,2,1,0:T(2,128)(2,1)S(1)}, bf16[1,16,64,2,512]{4,3,2,1,0:T(2,128)(2,1)}, u32[]{:S(2)}) copy-start(bf16[1,16,64,2,512]{4,3,2,1,0:T(2,128)(2,1)} %param.24) | copy-start | bytes 6291460
  103.7 22.1 %collective-permute-start.2 = (bf16[192,1,2304]{2,0,1:T(8,128)(2,1)}, bf16[192,1,2304]{2,0,1:T(8,128)(2,1)}, u32[]{:S(2)}, u32[]{:S(2)}) collective-permute-start(bf16[192,1,2304]{2,0,1:T(8,128)(2,1)} %bitcast.36), channel_id=1, source_target_pairs={{0,8},{8,0},{16,24},{24,16},{1,9},{9,1},{17,25},{25,17},{2,10},{10... | collective-permute-start | bytes 2654216 | tf_op jit(solution)/shard_map/ppermute | solution.py:134
  105.2 21.8 %collective-permute-start.3 = (bf16[192,1,2304]{2,0,1:T(8,128)(2,1)}, bf16[192,1,2304]{2,0,1:T(8,128)(2,1)}, u32[]{:S(2)}, u32[]{:S(2)}) collective-permute-start(bf16[192,1,2304]{2,0,1:T(8,128)(2,1)} %bitcast.36), channel_id=1, source_target_pairs={{0,16},{8,24},{16,0},{24,8},{1,17},{9,25},{17,1},{25,9},{2,18},{10... | collective-permute-start | bytes 2654216 | tf_op jit(solution)/shard_map/ppermute | solution.py:134
  127.0 11.7 %slice-start.2 = ((s8[13271040]{0:T(1024)(128)(4,1)}), s8[4194304]{0:T(1024)(128)(4,1)S(1)}, s32[]{:S(2)}) async-start(s8[13271040]{0:T(1024)(128)(4,1)} %bitcast.197), calls=%async_computation.11 | async-start | bytes 8388608
  128.7 10.0 %slice-start.3 = ((s8[13271040]{0:T(1024)(128)(4,1)}), s8[4194304]{0:T(1024)(128)(4,1)S(1)}, s32[]{:S(2)}) async-start(s8[13271040]{0:T(1024)(128)(4,1)} %bitcast.197), calls=%async_computation.12 | async-start | bytes 8388608
  128.7 10.0 %slice-start.4 = ((s8[13271040]{0:T(1024)(128)(4,1)}), s8[4194304]{0:T(1024)(128)(4,1)S(1)}, s32[]{:S(2)}) async-start(s8[13271040]{0:T(1024)(128)(4,1)} %bitcast.197), calls=%async_computation.13 | async-start | bytes 8388608
  128.8 10.0 %slice-start.5 = ((s8[13271040]{0:T(1024)(128)(4,1)}), s8[688128]{0:T(1024)(128)(4,1)S(1)}, s32[]{:S(2)}) async-start(s8[13271040]{0:T(1024)(128)(4,1)} %bitcast.197), calls=%async_computation.14 | async-start | bytes 1376256
  143.1 32.1 %collective-permute-start.4 = (bf16[192,1,2304]{2,0,1:T(8,128)(2,1)}, bf16[192,1,2304]{2,0,1:T(8,128)(2,1)}, u32[]{:S(2)}, u32[]{:S(2)}) collective-permute-start(bf16[192,1,2304]{2,0,1:T(8,128)(2,1)} %get-tuple-element.18), channel_id=1, source_target_pairs={{0,8},{8,0},{16,24},{24,16},{1,9},{9,1},{17,25},{25,17},{2,10},{10... | collective-permute-start | bytes 2654216 | tf_op jit(solution)/shard_map/ppermute | solution.py:134
  143.6 48.5 %collective-permute-start.5 = (bf16[192,1,2304]{2,0,1:T(8,128)(2,1)}, bf16[192,1,2304]{2,0,1:T(8,128)(2,1)}, u32[]{:S(2)}, u32[]{:S(2)}) collective-permute-start(bf16[192,1,2304]{2,0,1:T(8,128)(2,1)} %get-tuple-element.17), channel_id=1, source_target_pairs={{0,16},{8,24},{16,0},{24,8},{1,17},{9,25},{17,1},{25,9},{2,18},{10... | collective-permute-start | bytes 2654216 | tf_op jit(solution)/shard_map/ppermute | solution.py:134
  145.1 63.1 %collective-permute-start.6 = (bf16[192,1,2304]{2,0,1:T(8,128)(2,1)}, bf16[192,1,2304]{2,0,1:T(8,128)(2,1)}, u32[]{:S(2)}, u32[]{:S(2)}) collective-permute-start(bf16[192,1,2304]{2,0,1:T(8,128)(2,1)} %collective-permute-done.2), channel_id=1, source_target_pairs={{0,16},{8,24},{16,0},{24,8},{1,17},{9,25},{17,1},{25,9},{2,18},{10... | collective-permute-start | bytes 2654216 | tf_op jit(solution)/shard_map/ppermute | solution.py:134
  206.4 10.2 %slice-start.6 = ((s8[13271040]{0:T(1024)(128)(4,1)}), s8[4194304]{0:T(1024)(128)(4,1)S(1)}, s32[]{:S(2)}) async-start(s8[13271040]{0:T(1024)(128)(4,1)} %bitcast.199), calls=%async_computation.15 | async-start | bytes 8388608
  206.4 14.9 %slice-start = ((s8[4718592]{0:T(1024)(128)(4,1)}), s8[4194304]{0:T(1024)(128)(4,1)S(1)}, s32[]{:S(2)}) async-start(s8[4718592]{0:T(1024)(128)(4,1)} %bitcast.184), calls=%async_computation.9 | async-start | bytes 8388608
  208.2 9.0 %slice-start.9 = ((s8[13271040]{0:T(1024)(128)(4,1)}), s8[688128]{0:T(1024)(128)(4,1)S(1)}, s32[]{:S(2)}) async-start(s8[13271040]{0:T(1024)(128)(4,1)} %bitcast.199), calls=%async_computation.18 | async-start | bytes 1376256
  208.2 13.1 %slice-start.1 = ((s8[4718592]{0:T(1024)(128)(4,1)}), s8[524288]{0:T(1024)(128)(4,1)S(1)}, s32[]{:S(2)}) async-start(s8[4718592]{0:T(1024)(128)(4,1)} %bitcast.184), calls=%async_computation.10 | async-start | bytes 1048576
  218.9 22.8 %collective-permute-start.7 = (bf16[192,1,2304]{2,0,1:T(8,128)(2,1)S(1)}, bf16[192,1,2304]{2,0,1:T(8,128)(2,1)}, u32[]{:S(2)}, u32[]{:S(2)}) collective-permute-start(bf16[192,1,2304]{2,0,1:T(8,128)(2,1)S(1)} %fusion.39), channel_id=1, source_target_pairs={{0,24},{8,16},{16,8},{24,0},{1,25},{9,17},{17,9},{25,1},{2,26},{10... | collective-permute-start | bytes 2654216 | tf_op jit(solution)/shard_map/ppermute | solution.py:134
  266.0 29.2 %all-to-all-start.5 = ((bf16[16,64,2,512]{3,1,2,0:T(8,128)(2,1)}), bf16[16,64,2,512]{3,1,2,0:T(8,128)(2,1)S(1)}, u32[]{:S(2)}, u32[]{:S(2)}) async-start(bf16[16,64,2,512]{3,1,2,0:T(8,128)(2,1)} %broadcast_select_fusion.1), calls=%async_computation.6 | async-start | bytes 4194304 | tf_op jit(solution)/shard_map/all_to_all | solution.py:208
  (7 other events, 37.9 us)
Sparse Core Ops, SparseCore 0:
  37.9 57.9 all-reduce.1
  264.5 28.7 reduce-scatter.1
where the time goes:
time: 313 us; the launch traced here: 311 us
  waiting for transfers between devices  113 us (36%)
  matrix products  55.9 us (18%)
  local copies, waits for them, and re-layouts  52.6 us (17%)
  blocking collectives  31.1 us (10%)
  other arithmetic  27.7 us (9%)
  starting transfers between devices  16.9 us (5%)
  between operations  14.5 us (5%)
    psum x1, waiting for transfers between devices, body(): lax.psum(partial_value.astype(jnp.bfloat16), 'head').astype(jnp.float32)  55.2 us
    unnamed x54, local copies, waits for them, and re-layouts  40.4 us
    ppermute x6, waiting for transfers between devices, partner_move(): return lax.ppermute(block, 'req', [(i, i ^ step) for i in range(req_total)])  32.2 us
    dot_general x3, matrix products, experts_on(): jnp.einsum('ned,egdf->gnef', flat, gate_up_here, preferred_element_type=j...  25.9 us
    all_to_all x4, blocking collectives, body(): part = lax.all_to_all(part, 'dev', split_axis=0, concat_axis=1, tiled=True)  25.8 us
    all_to_all x1, waiting for transfers between devices, body(): lax.all_to_all(outgoing, 'req', split_axis=0, concat_axis=0, tiled=True)  25.1 us
    dot_general x4, matrix products, body(): jnp.einsum('tec,ced->ted', dispatch_bf, part, preferred_element_type=jnp....  11.2 us
    ppermute x3, other arithmetic, partner_move(): return lax.ppermute(block, 'req', [(i, i ^ step) for i in range(req_total)])  9.36 us
  transfers between devices with their start and end apart: 11, of which 5 were waited for; matrix products, arithmetic and copies ran while one was open for 22% of the time, Pallas kernels for 0%

commit v1 on v0

--- a/solution.py
+++ b/solution.py
@@ -1,3 +1,4 @@
+import functools
 import jax
 import jax.numpy as jnp
 from jax import lax
@@ -5,6 +6,19 @@
 
 EXPERTS = 8
 HD = 64
+
+
+def order_the_quarters(matrix, comm_axis):
+    t_next = lax.all_to_all(
+        jnp.stack(jnp.split(matrix, lax.axis_size(comm_axis), 0), 0),
+        axis_name=comm_axis,
+        split_axis=0,
+        concat_axis=0,
+    )
+    return jnp.concatenate(t_next, axis=1)
+
+
+slot_draft = functools.partial(order_the_quarters, comm_axis="dev")
 
 
 def shifted(block, axis, distance):
@@ -158,7 +172,7 @@
             part = outs[slot_index]
             part = part if step == 0 else partner_move(part, step)
             if split:
-                part = lax.all_to_all(part, "dev", split_axis=0, concat_axis=1, tiled=True)
+                part = slot_draft(part)
             returned.append(part)
     token_weights = jnp.sum(own_combine, axis=-1)
     dispatch_bf = own_dispatch.astype(jnp.bfloat16)

time: 313 us -> 270 us (0.86)
  local copies, waits for them, and re-layouts: 52.6 us -> 28.2 us
  blocking collectives: 31.1 us -> 13.5 us
  other arithmetic: 27.7 us -> 17.8 us
  starting transfers between devices: 16.9 us -> 24.9 us
    unnamed x54 -> x28, local copies, waits for them, and re-layouts: 40.4 us -> 14.4 us
    all_to_all x4 -> x2, blocking collectives: 25.8 us -> 8.85 us  [order_the_quarters(): lax.all_to_all(jnp.stack(jnp.split(matrix, lax.axis_size(comm_axis), 0),...]
    ppermute x3 -> x0, other arithmetic: 9.36 us -> none  [partner_move(): return lax.ppermute(block, 'req', [(i, i ^ step) for i in range(req_total)])]
    all_to_all x0 -> x2, starting transfers between devices: none -> 8.93 us  [order_the_quarters(): lax.all_to_all(jnp.stack(jnp.split(matrix, lax.axis_size(comm_axis), 0),...]
    ppermute x6, waiting for transfers between devices: 32.2 us -> 37.9 us  [partner_move(): return lax.ppermute(block, 'req', [(i, i ^ step) for i in range(req_total)])]
    psum x1, waiting for transfers between devices: 55.2 us -> 49.4 us  [body(): lax.psum(partial_value.astype(jnp.bfloat16), 'head').astype(jnp.float32)]
    convert_element_type x1 -> x0, other arithmetic: 3.13 us -> none  [experts_on(): return down.astype(jnp.bfloat16).reshape(rows.shape)]
  transfers between devices with their start and end apart: 11 -> 13, of which waited for: 5 -> 6; matrix products, arithmetic and copies ran while one was open for 22% -> 23% of each run, Pallas kernels for 0% -> 0%
where the time goes in v1:
time: 270 us; the launch traced here: 269 us
  waiting for transfers between devices  113 us (42%)
  matrix products  57.4 us (21%)
  local copies, waits for them, and re-layouts  28.2 us (10%)
  starting transfers between devices  24.9 us (9%)
  other arithmetic  17.8 us (7%)
  between operations  14.5 us (5%)
  blocking collectives  13.5 us (5%)
    psum x1, waiting for transfers between devices, body(): lax.psum(partial_value.astype(jnp.bfloat16), 'head').astype(jnp.float32)  49.4 us
    ppermute x6, waiting for transfers between devices, partner_move(): return lax.ppermute(block, 'req', [(i, i ^ step) for i in range(req_total)])  37.9 us
    all_to_all x1, waiting for transfers between devices, body(): lax.all_to_all(outgoing, 'req', split_axis=0, concat_axis=0, tiled=True)  25.1 us
    dot_general x3, matrix products, experts_on(): jnp.einsum('ned,egdf->gnef', flat, gate_up_here, preferred_element_type=j...  24.7 us
    unnamed x28, local copies, waits for them, and re-layouts  14.4 us
    dot_general x4, matrix products, body(): jnp.einsum('tec,ced->ted', dispatch_bf, part, preferred_element_type=jnp....  13.9 us
    all_to_all x2, starting transfers between devices, order_the_quarters(): lax.all_to_all(jnp.stack(jnp.split(matrix, lax.axis_size(comm_axis), 0),...  8.93 us
    all_to_all x2, blocking collectives, order_the_quarters(): lax.all_to_all(jnp.stack(jnp.split(matrix, lax.axis_size(comm_axis), 0),...  8.85 us
  transfers between devices with their start and end apart: 13, of which 6 were waited for; matrix products, arithmetic and copies ran while one was open for 23% of the time, Pallas kernels for 0%

profile of v1, /device:TPU:0, one launch (start us, length us, event | category | flops | bytes accessed | tf_op | source)
XLA Modules:
  0.0 268.8 jit_solution(8197546861257384548)
XLA Ops:
  7.3 10.3 %copy.37 = bf16[2304,3,512]{0,2,1:T(8,128)(2,1)} copy(bf16[2304,3,512]{2,0,1:T(8,128)(2,1)} %param.17) | data formatting | bytes 14155776 | tf_op args[2]
  17.9 5.2 %fusion.68 = f32[256,3,8,64]{0,3,2,1:T(8,128)S(1)} fusion(bf16[3,8,64,2304]{3,2,1,0:T(8,128)(2,1)} %bitcast.196, bf16[1,256,2304]{2,1,0:T(8,128)(2,1)S(1)} %copy-done.2, f32[2304]{0:T(1024)} %param.16, f32[256]{0:T(256)S(1)} %add_rsqrt_fusion.1), kind=kOutput, calls=%fused_computation.64 | convolution fusion | flops 1814298624 | bytes 9840640 | tf_op jit(solution)/shard_map/dot_general | solution.py:87
  23.5 3.1 %collective-permute-start.1 = (bf16[256,8,64]{0,2,1:T(8,128)(2,1)S(1)}, bf16[256,8,64]{0,2,1:T(8,128)(2,1)}, u32[]{:S(2)}, u32[]{:S(2)}) collective-permute-start(bf16[256,8,64]{0,2,1:T(8,128)(2,1)S(1)} %pad_maximum_fusion.5), channel_id=1, source_target_pairs={{0,1},{2,3},{4,5},{6,7},{8,9},{10,11},{12,13},{14,15},{16,17},{18,... | collective-permute-start | bytes 786440 | tf_op jit(solution)/shard_map/ppermute | solution.py:27
  40.9 3.2 %bitcast_select_fusion = bf16[16,64,2,512]{3,1,2,0:T(8,128)(2,1)} fusion(bf16[1,16,64,2,512]{4,3,2,1,0:T(2,128)(2,1)} %param.24, pred[16,64]{1,0:T(8,128)(4,1)S(1)} %add_compare_fusion), kind=kLoop, calls=%fused_computation.55 | loop fusion | flops 1048576 | bytes 4195328 | tf_op jit(solution)/shard_map/jit(_where)/select_n | solution.py:218
  47.9 49.4 %all-reduce.2.cloned.1.call-done = bf16[256,2304]{1,0:T(8,128)(2,1)} async-done(((bf16[256,2304]{1,0:T(8,128)(2,1)}), bf16[256,2304]{1,0:T(8,128)(2,1)}) %all-reduce.2.cloned.1.call-update) | async-done | bytes 1179664 | tf_op jit(solution)/shard_map/psum | solution.py:118
  100.1 4.7 %all_to_all.43 = bf16[96,2,2304]{2,0,1:T(8,128)(2,1)S(1)} all-to-all(bf16[96,2,2304]{2,0,1:T(8,128)(2,1)S(1)} %convert_bitcast_fusion.1), channel_id=1, replica_groups=mesh['req'=4,'head'=4,'dev'=2] {'dev'}, dimensions={1} | all-to-all | bytes 1769472 | tf_op jit(solution)/shard_map/all_to_all | solution.py:143
  107.8 7.6 %fusion.44 = f32[2,192,1,1440]{3,1,0,2:T(8,128)S(1)} fusion(bf16[192,2304,1]{1,0,2:T(8,128)(2,1)S(1)} %bitcast.204, bf16[2,2,2304,1440]{2,3,1,0:T(8,128)(2,1)} %param.22, s32[]{:T(128)S(6)} %select_n.44), kind=kOutput, calls=%fused_computation.38 | convolution fusion | flops 2548039680 | bytes 16367620 | tf_op jit(solution)/shard_map/ned,egdf->gnef/dot_general | solution.py:153
  117.2 4.4 %all_to_all.44 = bf16[2,96,1,2304]{3,1,2,0:T(8,128)(2,1)S(1)} all-to-all(bf16[2,96,1,2304]{3,1,2,0:T(8,128)(2,1)S(1)} %pad_maximum_fusion.1), channel_id=1, replica_groups=mesh['req'=4,'head'=4,'dev'=2] {'dev'}, dimensions={0} | all-to-all | bytes 1769472 | tf_op jit(solution)/shard_map/all_to_all | solution.py:12
  121.7 2.9 %fusion.89 = f32[2,2304,256]{2,1,0:T(8,128)} fusion(bf16[256,2,96]{0,2,1:T(8,128)(2,1)S(1)} %get-tuple-element.12, bf16[2,96,1,2304]{3,1,2,0:T(8,128)(2,1)S(1)} %all_to_all.44), kind=kOutput, calls=%fused_computation.84 | convolution fusion | flops 226492416 | bytes 5701632 | tf_op jit(solution)/shard_map/tec,ced->ted/dot_general | solution.py:181
  127.9 9.7 %fusion.26 = f32[2,384,1,1440]{1,3,0,2:T(8,128)S(1)} fusion(bf16[384,2304,1]{1,0,2:T(8,128)(2,1)S(1)} %bitcast.199, bf16[2,2,2304,1440]{2,3,1,0:T(8,128)(2,1)} %param.22, s32[]{:T(128)S(6)} %select_n.44), kind=kOutput, calls=%fused_computation.30 | convolution fusion | flops 5096079360 | bytes 19464196 | tf_op jit(solution)/shard_map/ned,egdf->gnef/dot_general | solution.py:153
  139.2 3.0 %fusion.23 = bf16[384,1,2304]{2,0,1:T(8,128)(2,1)S(1)} fusion(bf16[2,1440,2304]{2,1,0:T(8,128)(2,1)S(1)} %bitcast.209, s32[]{:T(128)S(6)} %select_n.44, f32[2,384,1,1440]{1,3,0,2:T(8,128)S(1)} %fusion.26), kind=kOutput, calls=%fused_computation.28 | convolution fusion | flops 2552242176 | bytes 12828676 | tf_op jit(solution)/shard_map/nef,efd->ned/dot_general | solution.py:155
  144.3 16.0 %collective-permute-done.6 = bf16[192,1,2304]{2,0,1:T(8,128)(2,1)S(1)} collective-permute-done((bf16[192,1,2304]{2,0,1:T(8,128)(2,1)S(1)}, bf16[192,1,2304]{2,0,1:T(8,128)(2,1)S(1)}, u32[]{:S(2)}, u32[]{:S(2)}) %collective-permute-start.6) | collective-permute-done | bytes 884768 | tf_op jit(solution)/shard_map/ppermute | solution.py:148
  160.3 7.4 %fusion.47 = f32[2,192,1,1440]{3,1,0,2:T(8,128)S(1)} fusion(bf16[2,2,2304,1440]{2,3,1,0:T(8,128)(2,1)} %param.22, s32[]{:T(128)S(6)} %select_n.44, bf16[192,1,2304]{2,0,1:T(8,128)(2,1)S(1)} %collective-permute-done.6), kind=kOutput, calls=%fused_computation.39 | convolution fusion | flops 2548039680 | bytes 16367620 | tf_op jit(solution)/shard_map/ned,egdf->gnef/dot_general | solution.py:153
  167.7 2.6 fusion.39
  172.9 4.6 %all-to-all-start.2 = ((bf16[2,96,1,2304]{3,1,2,0:T(8,128)(2,1)}), bf16[2,96,1,2304]{3,1,2,0:T(8,128)(2,1)}, u32[]{:S(2)}, u32[]{:S(2)}) async-start(bf16[2,96,1,2304]{3,1,2,0:T(8,128)(2,1)} %pad_maximum_fusion.2), calls=%async_computation.2 | async-start | bytes 1769472 | tf_op jit(solution)/shard_map/all_to_all | solution.py:12
  177.5 18.8 %collective-permute-done.5 = bf16[192,1,2304]{2,0,1:T(8,128)(2,1)} collective-permute-done((bf16[192,1,2304]{2,0,1:T(8,128)(2,1)}, bf16[192,1,2304]{2,0,1:T(8,128)(2,1)}, u32[]{:S(2)}, u32[]{:S(2)}) %collective-permute-start.5) | collective-permute-done | bytes 884768 | tf_op jit(solution)/shard_map/ppermute | solution.py:148
  198.5 4.3 %all-to-all-start.3 = ((bf16[2,96,1,2304]{3,1,2,0:T(8,128)(2,1)}), bf16[2,96,1,2304]{3,1,2,0:T(8,128)(2,1)}, u32[]{:S(2)}, u32[]{:S(2)}) async-start(bf16[2,96,1,2304]{3,1,2,0:T(8,128)(2,1)} %pad_maximum_fusion.3), calls=%async_computation.3 | async-start | bytes 1769472 | tf_op jit(solution)/shard_map/all_to_all | solution.py:12
  202.9 5.6 %convolution_add_fusion.2 = f32[2,2304,256]{2,1,0:T(8,128)} fusion(f32[2,2304,256]{2,1,0:T(8,128)} %fusion.89, bf16[256,2,96]{0,2,1:T(8,128)(2,1)S(1)} %get-tuple-element.12, bf16[2,96,1,2304]{3,1,2,0:T(8,128)(2,1)} %all-to-all-done.2), kind=kOutput, calls=%fused_computation.19 | convolution fusion | flops 227672064 | bytes 10420224 | tf_op jit(solution)/shard_map/tec,ced->ted/dot_general | solution.py:181
  208.5 3.4 %convolution_add_fusion.1 = f32[2,2304,256]{2,1,0:T(8,128)S(1)} fusion(f32[2,2304,256]{2,1,0:T(8,128)} %convolution_add_fusion.2, bf16[256,2,96]{0,2,1:T(8,128)(2,1)S(1)} %get-tuple-element.12, bf16[2,96,1,2304]{3,1,2,0:T(8,128)(2,1)} %all-to-all-done.3), kind=kOutput, calls=%fused_computation.18 | convolution fusion | flops 227672064 | bytes 10420224 | tf_op jit(solution)/shard_map/tec,ced->ted/dot_general | solution.py:181
  213.3 4.4 %all_to_all.45 = bf16[2,96,1,2304]{3,1,2,0:T(8,128)(2,1)S(1)} all-to-all(bf16[2,96,1,2304]{3,1,2,0:T(8,128)(2,1)S(1)} %pad_maximum_fusion.4), channel_id=1, replica_groups=mesh['req'=4,'head'=4,'dev'=2] {'dev'}, dimensions={0} | all-to-all | bytes 1769472 | tf_op jit(solution)/shard_map/all_to_all | solution.py:12
  219.6 2.4 copy.40
  223.6 3.8 %all-to-all-start.5 = ((bf16[16,64,2,512]{3,1,2,0:T(8,128)(2,1)}), bf16[16,64,2,512]{3,1,2,0:T(8,128)(2,1)S(1)}, u32[]{:S(2)}, u32[]{:S(2)}) async-start(bf16[16,64,2,512]{3,1,2,0:T(8,128)(2,1)} %broadcast_select_fusion.1), calls=%async_computation.6 | async-start | bytes 4194304 | tf_op jit(solution)/shard_map/all_to_all | solution.py:222
  227.6 25.1 %all-to-all-done.5 = bf16[16,64,2,512]{3,1,2,0:T(8,128)(2,1)S(1)} async-done(((bf16[16,64,2,512]{3,1,2,0:T(8,128)(2,1)}), bf16[16,64,2,512]{3,1,2,0:T(8,128)(2,1)S(1)}, u32[]{:S(2)}, u32[]{:S(2)}) %all-to-all-start.5) | async-done | bytes 2097184 | tf_op jit(solution)/shard_map/all_to_all | solution.py:222
  256.8 3.5 %copy.42 = bf16[16,64,2,512]{3,2,1,0:T(2,128)(2,1)} copy(bf16[16,64,2,512]{3,1,2,0:T(8,128)(2,1)S(1)} %broadcast_select_fusion) | data formatting | bytes 4194304
  (122 shorter events, 48.9 us)
Async XLA Ops:
  7.2 30.2 %copy-start = (bf16[512,2304]{1,0:T(8,128)(2,1)S(1)}, bf16[512,2304]{1,0:T(8,128)(2,1)}, u32[]{:S(2)}) copy-start(bf16[512,2304]{1,0:T(8,128)(2,1)} %param.18) | copy-start | bytes 7077892
  7.2 90.2 %all-reduce.2.cloned.1.call-start = ((), (), s32[]{:S(2)}) async-start(), calls=%async_computation.7 | async-start | bytes 2359296 | tf_op jit(solution)/shard_map/psum | solution.py:118
  7.3 10.3 %copy-start.2 = (bf16[1,256,2304]{2,1,0:T(8,128)(2,1)S(1)}, bf16[1,256,2304]{2,1,0:T(8,128)(2,1)}, u32[]{:S(2)}) copy-start(bf16[1,256,2304]{2,1,0:T(8,128)(2,1)} %param.15) | copy-start | bytes 3538948
  23.1 7.7 %copy-start.3 = (s32[4,16]{1,0:T(4,128)S(1)}, s32[4,16]{1,0:T(4,128)}, u32[]{:S(2)}) copy-start(s32[4,16]{1,0:T(4,128)} %param.26) | copy-start | bytes 772
  23.5 8.4 %collective-permute-start.1 = (bf16[256,8,64]{0,2,1:T(8,128)(2,1)S(1)}, bf16[256,8,64]{0,2,1:T(8,128)(2,1)}, u32[]{:S(2)}, u32[]{:S(2)}) collective-permute-start(bf16[256,8,64]{0,2,1:T(8,128)(2,1)S(1)} %pad_maximum_fusion.5), channel_id=1, source_target_pairs={{0,1},{2,3},{4,5},{6,7},{8,9},{10,11},{12,13},{14,15},{16,17},{18,... | collective-permute-start | bytes 786440 | tf_op jit(solution)/shard_map/ppermute | solution.py:27
  26.6 8.5 %collective-permute-start = (bf16[256,8,64]{0,2,1:T(8,128)(2,1)S(1)}, bf16[256,8,64]{0,2,1:T(8,128)(2,1)}, u32[]{:S(2)}, u32[]{:S(2)}) collective-permute-start(bf16[256,8,64]{0,2,1:T(8,128)(2,1)S(1)} %fusion.107), channel_id=1, source_target_pairs={{0,1},{2,3},{4,5},{6,7},{8,9},{10,11},{12,13},{14,15},{16,17},{18,... | collective-permute-start | bytes 786440 | tf_op jit(solution)/shard_map/ppermute | solution.py:27
  46.4 53.1 %copy-start.4 = (f32[2304]{0:T(1024)S(1)}, f32[2304]{0:T(1024)}, u32[]{:S(2)}) copy-start(f32[2304]{0:T(1024)} %param.19) | copy-start | bytes 27652
  100.1 15.2 %slice-start = ((s8[13271040]{0:T(1024)(128)(4,1)}), s8[4194304]{0:T(1024)(128)(4,1)S(1)}, s32[]{:S(2)}) async-start(s8[13271040]{0:T(1024)(128)(4,1)} %bitcast.208), calls=%async_computation.9 | async-start | bytes 8388608
  104.8 21.7 %collective-permute-start.2 = (bf16[192,1,2304]{2,0,1:T(8,128)(2,1)S(1)}, bf16[192,1,2304]{2,0,1:T(8,128)(2,1)S(1)}, u32[]{:S(2)}, u32[]{:S(2)}) collective-permute-start(bf16[192,1,2304]{2,0,1:T(8,128)(2,1)S(1)} %bitcast.202), channel_id=1, source_target_pairs={{0,8},{8,0},{16,24},{24,16},{1,9},{9,1},{17,25},{25,17},{2,10},{10... | collective-permute-start | bytes 2654216 | tf_op jit(solution)/shard_map/ppermute | solution.py:148
  106.3 21.5 %collective-permute-start.3 = (bf16[192,1,2304]{2,0,1:T(8,128)(2,1)S(1)}, bf16[192,1,2304]{2,0,1:T(8,128)(2,1)S(1)}, u32[]{:S(2)}, u32[]{:S(2)}) collective-permute-start(bf16[192,1,2304]{2,0,1:T(8,128)(2,1)S(1)} %bitcast.203), channel_id=1, source_target_pairs={{0,16},{8,24},{16,0},{24,8},{1,17},{9,25},{17,1},{25,9},{2,18},{10... | collective-permute-start | bytes 2654216 | tf_op jit(solution)/shard_map/ppermute | solution.py:148
  107.8 7.6 %slice-start.1 = ((s8[13271040]{0:T(1024)(128)(4,1)}), s8[4194304]{0:T(1024)(128)(4,1)S(1)}, s32[]{:S(2)}) async-start(s8[13271040]{0:T(1024)(128)(4,1)} %bitcast.208), calls=%async_computation.10 | async-start | bytes 8388608
  107.8 7.6 %slice-start.2 = ((s8[13271040]{0:T(1024)(128)(4,1)}), s8[4194304]{0:T(1024)(128)(4,1)S(1)}, s32[]{:S(2)}) async-start(s8[13271040]{0:T(1024)(128)(4,1)} %bitcast.208), calls=%async_computation.11 | async-start | bytes 8388608
  107.8 7.6 %slice-start.3 = ((s8[13271040]{0:T(1024)(128)(4,1)}), s8[688128]{0:T(1024)(128)(4,1)S(1)}, s32[]{:S(2)}) async-start(s8[13271040]{0:T(1024)(128)(4,1)} %bitcast.208), calls=%async_computation.12 | async-start | bytes 1376256
  137.6 22.7 %collective-permute-start.6 = (bf16[192,1,2304]{2,0,1:T(8,128)(2,1)S(1)}, bf16[192,1,2304]{2,0,1:T(8,128)(2,1)S(1)}, u32[]{:S(2)}, u32[]{:S(2)}) collective-permute-start(bf16[192,1,2304]{2,0,1:T(8,128)(2,1)S(1)} %collective-permute-done.2), channel_id=1, source_target_pairs={{0,16},{8,24},{16,0},{24,8},{1,17},{9,25},{17,1},{25,9},{2,18},{10... | collective-permute-start | bytes 2654216 | tf_op jit(solution)/shard_map/ppermute | solution.py:148
  143.2 53.1 %collective-permute-start.5 = (bf16[192,1,2304]{2,0,1:T(8,128)(2,1)}, bf16[192,1,2304]{2,0,1:T(8,128)(2,1)}, u32[]{:S(2)}, u32[]{:S(2)}) collective-permute-start(bf16[192,1,2304]{2,0,1:T(8,128)(2,1)} %get-tuple-element.15), channel_id=1, source_target_pairs={{0,16},{8,24},{16,0},{24,8},{1,17},{9,25},{17,1},{25,9},{2,18},{10... | collective-permute-start | bytes 2654216 | tf_op jit(solution)/shard_map/ppermute | solution.py:148
  143.8 28.1 %collective-permute-start.4 = (bf16[192,1,2304]{2,0,1:T(8,128)(2,1)S(1)}, bf16[192,1,2304]{2,0,1:T(8,128)(2,1)S(1)}, u32[]{:S(2)}, u32[]{:S(2)}) collective-permute-start(bf16[192,1,2304]{2,0,1:T(8,128)(2,1)S(1)} %get-tuple-element.16), channel_id=1, source_target_pairs={{0,8},{8,0},{16,24},{24,16},{1,9},{9,1},{17,25},{25,17},{2,10},{10... | collective-permute-start | bytes 2654216 | tf_op jit(solution)/shard_map/ppermute | solution.py:148
  170.3 41.6 %collective-permute-start.7 = (bf16[192,1,2304]{2,0,1:T(8,128)(2,1)}, bf16[192,1,2304]{2,0,1:T(8,128)(2,1)}, u32[]{:S(2)}, u32[]{:S(2)}) collective-permute-start(bf16[192,1,2304]{2,0,1:T(8,128)(2,1)} %fusion.39), channel_id=1, source_target_pairs={{0,24},{8,16},{16,8},{24,0},{1,25},{9,17},{17,9},{25,1},{2,26},{10... | collective-permute-start | bytes 2654216 | tf_op jit(solution)/shard_map/ppermute | solution.py:148
  172.9 25.6 %all-to-all-start.2 = ((bf16[2,96,1,2304]{3,1,2,0:T(8,128)(2,1)}), bf16[2,96,1,2304]{3,1,2,0:T(8,128)(2,1)}, u32[]{:S(2)}, u32[]{:S(2)}) async-start(bf16[2,96,1,2304]{3,1,2,0:T(8,128)(2,1)} %pad_maximum_fusion.2), calls=%async_computation.2 | async-start | bytes 1769472 | tf_op jit(solution)/shard_map/all_to_all | solution.py:12
  198.5 10.0 %all-to-all-start.3 = ((bf16[2,96,1,2304]{3,1,2,0:T(8,128)(2,1)}), bf16[2,96,1,2304]{3,1,2,0:T(8,128)(2,1)}, u32[]{:S(2)}, u32[]{:S(2)}) async-start(bf16[2,96,1,2304]{3,1,2,0:T(8,128)(2,1)} %pad_maximum_fusion.3), calls=%async_computation.3 | async-start | bytes 1769472 | tf_op jit(solution)/shard_map/all_to_all | solution.py:12
  202.9 57.4 %reduce-scatter.2.cloned.1.call-start = ((), (), s32[]{:S(2)}) async-start(), calls=%async_computation.8 | async-start | bytes 1474560 | tf_op jit(solution)/shard_map/reduce_scatter | solution.py:186
  219.6 2.4 copy-start.8
  223.6 3.9 %copy-start.5 = (s32[4,16]{1,0:T(4,128)S(1)}, s32[4,16]{1,0:T(4,128)}, u32[]{:S(2)}) copy-start(s32[4,16]{1,0:T(4,128)} %param.27) | copy-start | bytes 772
  223.6 29.2 %all-to-all-start.5 = ((bf16[16,64,2,512]{3,1,2,0:T(8,128)(2,1)}), bf16[16,64,2,512]{3,1,2,0:T(8,128)(2,1)S(1)}, u32[]{:S(2)}, u32[]{:S(2)}) async-start(bf16[16,64,2,512]{3,1,2,0:T(8,128)(2,1)} %broadcast_select_fusion.1), calls=%async_computation.6 | async-start | bytes 4194304 | tf_op jit(solution)/shard_map/all_to_all | solution.py:222
  254.8 7.2 %copy-start.1 = (bf16[512,2304]{1,0:T(8,128)(2,1)S(1)}, bf16[512,2304]{1,0:T(8,128)(2,1)}, u32[]{:S(2)}) copy-start(bf16[512,2304]{1,0:T(8,128)(2,1)} %param.18) | copy-start | bytes 7077892
  (2 other events, 2.8 us)
Sparse Core Ops, SparseCore 0:
  39.3 57.9 all-reduce.1
  222.1 27.9 reduce-scatter.1
